TPU v7x, 32 devices: a whole 2x2x4 slice. The times are simulated.
32 devices in a mesh: dp: 4 (over y, x), expert: 8 (over z, core).
Axes of the slice: x: 2, y: 2, z: 4, core: 2. Of those that a mesh axis runs over, the one named last changes fastest.
Arguments:
- hidden: bfloat16 [32, 2048], P(('dp', 'expert')), may hold values from -6 to 6
- attn_gain: float32 [2048], replicated, may hold values from 0.25 to 1.75
- query_weight: bfloat16 [3072, 2048], P('expert'), may hold values from -0.125 to 0.125
- latent_down: bfloat16 [2048, 576], replicated, may hold values from -0.125 to 0.125
- latent_up: bfloat16 [512, 4096], P(None, 'expert'), may hold values from -0.25 to 0.25
- out_weight: bfloat16 [2048, 2048], P('expert'), may hold values from -0.125 to 0.125
- latent_pool: bfloat16 [128, 32, 576], P('dp'), may hold values from -1000 to 1000
- page_table: int32 [32, 16], replicated, may hold values from -1 to 127, as said below
- page_counts: int32 [32], replicated, may hold values from 1 to 16, as said below
- ffn_gain: float32 [2048], replicated, may hold values from 0.25 to 1.75
- expert_ids: int32 [32, 6], replicated, may hold values from 0 to 23, all different within a row; in each aligned block of 32 rows (0 to 31, 32 to 63, ...) at most 16 rows name the same one
- expert_gates: float32 [32, 6], replicated, may hold values from 0.05 to 0.6
- old_place: int32 [8, 4], replicated, may hold values from 0 to 23, as said below
- new_place: int32 [8, 4], replicated, may hold values from 0 to 23, as said below
- expert_gate_up: bfloat16 [32, 2, 1408, 2048], P('expert', None, None, 'dp'), as said below
- expert_down: bfloat16 [32, 1408, 2048], P('expert', None, 'dp'), as said below
- shared_gate_up: bfloat16 [2, 2816, 2048], P(None, None, 'dp'), may hold values from -0.125 to 0.125
- shared_down: bfloat16 [2816, 2048], P(None, 'dp'), may hold values from -0.109375 to 0.109375
Outputs:
- layer_out: bfloat16 [32, 2048], P(('dp', 'expert'))
- moved_gate_up: bfloat16 [32, 2, 1408, 2048], P('expert', None, None, 'dp')
- moved_down: bfloat16 [32, 1408, 2048], P('expert', None, 'dp')
Inputs may be any that keep to these rules, and one draw needn't show every extreme that they name: `page_counts`: each request's count of cached pages; exactly one request has 16. `page_table`: row t names page_counts[t] pages of the pool, no page named twice in the table; its other entries are -1. Page p lies on dp index p // 32. `expert_ids`: no expert is named by more than 16 tokens in all; some expert by exactly 16. `old_place`: row i holds the experts of the slots on expert index i, slot s of row i being global slot i * 4 + s; every expert is held by one slot or more. `new_place`: equal to old_place except in exactly one slot of each row, which names another expert. `expert_gate_up`: slots that hold the same expert under old_place hold equal weights. `expert_down`: slots that hold the same expert under old_place hold equal weights.
All inputs are finite; a program needn't handle non-finite values.
Results may differ from a plain program's by a relative error of at most 0.02.
Values may be sent and summed in bfloat16 or wider, within the bound.
No kernel may reach another device: no remote copies, remote signals or barrier semaphores. Data moves between devices by JAX's collectives and lax.ppermute only.
A program may use at most 128 MiB of HBM per device.

v0:
```python
import math
import jax
import jax.numpy as jnp
from jax import lax
from jax.sharding import PartitionSpec as P

NOPE = 128
ROPE = 64
VHEAD = 128
LATENT = 512
EXP_DEV = 3
PAGE = 32
EPSILON = 1e-06
ROPE_BASE = 50000.0
MASKED_SCORE = -1e30
HIGHEST = lax.Precision.HIGHEST


def combined_all(part, axis, combine):
    gathered = jax.tree.map(lambda a: lax.all_gather(a, axis), part)

    def take(source):
        return jax.tree.map(lambda a: lax.dynamic_index_in_dim(a, source, 0, False), gathered)

    return lax.fori_loop(
        1, lax.axis_size(axis), lambda source, state: combine(state, take(source)), take(0)
    )


def rms_plain(values):
    mean_square = jnp.mean(values * values, axis=-1, keepdims=True)
    return values * lax.rsqrt(mean_square + EPSILON)


def rms_norm(values, norm_gain):
    return rms_plain(values) * norm_gain


def rotary(values, position):
    half_width = values.shape[-1] // 2
    exponent = jnp.arange(half_width).astype(jnp.float32) * (2.0 / values.shape[-1])
    frequency = jnp.exp(-exponent * math.log(ROPE_BASE))
    angles = position[..., None] * frequency
    cosine = jnp.cos(angles)
    sine_part = jnp.sin(angles)
    first_half = values[..., :half_width]
    second = values[..., half_width:]
    return jnp.concatenate(
        [first_half * cosine - second * sine_part, second * cosine + first_half * sine_part],
        axis=-1,
    )


def combine_parts(earlier, later):
    highest = jnp.maximum(earlier[0], later[0])
    weight_early = jnp.exp(earlier[0] - highest)
    weight_late = jnp.exp(later[0] - highest)
    return (
        highest,
        earlier[1] * weight_early + later[1] * weight_late,
        earlier[2] * weight_early[..., None] + later[2] * weight_late[..., None],
    )


def local(
    hidden,
    attn_gain,
    query_weight,
    latent_down,
    latent_up,
    out_weight,
    latent_pool,
    page_table,
    page_counts,
    ffn_gain,
    expert_ids,
    expert_gates,
    old_place,
    new_place,
    expert_gate_up,
    expert_down,
    shared_gate_up,
    shared_down,
):
    dp_count = lax.axis_size("dp")
    ex_count = lax.axis_size("expert")
    dp_index = lax.axis_index("dp")
    ex_index = lax.axis_index("expert")
    req_local = hidden.shape[0]
    group_rows = req_local * ex_count
    requests = page_counts.shape[0]
    head_local = query_weight.shape[0] // (NOPE + ROPE)
    score_scale = (NOPE + ROPE) ** (-0.5)
    group_start = dp_index * group_rows
    everyone = lax.all_gather(hidden, ("dp", "expert"), axis=0, tiled=True)
    normed = rms_norm(everyone.astype(jnp.float32), attn_gain).astype(jnp.bfloat16)
    queries = jnp.einsum(
        "td,qd->tq", normed, query_weight, preferred_element_type=jnp.float32
    ).reshape(requests, head_local, NOPE + ROPE)
    position = (page_counts * PAGE).astype(jnp.float32)
    query_rope = rotary(queries[..., NOPE:], position[:, None]).astype(jnp.bfloat16)
    up_table = latent_up.reshape(LATENT, head_local, NOPE + VHEAD)
    query_latent = jnp.einsum(
        "thn,lhn->thl",
        queries[..., :NOPE],
        up_table[..., :NOPE].astype(jnp.float32),
        precision=HIGHEST,
    ).astype(jnp.bfloat16)
    pages_local = latent_pool.shape[0]
    pool_total = pages_local * dp_count
    flat_pages = page_table.reshape(-1)
    flat_owner = jnp.repeat(jnp.arange(requests, dtype=jnp.int32), page_table.shape[1])
    target = jnp.where(flat_pages >= 0, flat_pages, pool_total)
    owner_all = jnp.full((pool_total,), -1, jnp.int32).at[target].set(flat_owner, mode="drop")
    page_owner = lax.dynamic_slice_in_dim(owner_all, dp_index * pages_local, pages_local)
    page_used = page_owner >= 0
    owner_safe = jnp.maximum(page_owner, 0)
    page_latent = latent_pool[..., :LATENT]
    page_rope = latent_pool[..., LATENT:]
    scores = jnp.einsum(
        "phl,pkl->phk", query_latent[owner_safe], page_latent, preferred_element_type=jnp.float32
    )
    scores = (
        scores
        + jnp.einsum(
            "phr,pkr->phk", query_rope[owner_safe], page_rope, preferred_element_type=jnp.float32
        )
    ) * score_scale
    raw_max = jnp.max(scores, axis=2)
    weights = jnp.exp(scores - raw_max[..., None])
    page_total = jnp.sum(weights, axis=2)
    page_mix = jnp.einsum(
        "phk,pkl->phl",
        weights.astype(jnp.bfloat16),
        page_latent,
        preferred_element_type=jnp.float32,
    )
    page_max = jnp.where(page_used[:, None], raw_max, MASKED_SCORE)
    member = page_owner[None, :] == jnp.arange(requests, dtype=jnp.int32)[:, None]
    req_max = jnp.max(jnp.where(member[:, :, None], page_max[None], MASKED_SCORE), axis=1)
    rescale = jnp.where(page_used[:, None], jnp.exp(page_max - req_max[owner_safe]), 0.0)
    member_float = member.astype(jnp.float32)
    req_total = jnp.dot(member_float, page_total * rescale, precision=HIGHEST)
    req_mix = jnp.einsum(
        "rp,phl->rhl", member_float, page_mix * rescale[..., None], precision=HIGHEST
    )
    merged = combined_all((req_max, req_total, req_mix), "dp", combine_parts)
    part_max = lax.dynamic_slice_in_dim(merged[0], group_start, group_rows, 0)
    part_total = lax.dynamic_slice_in_dim(merged[1], group_start, group_rows, 0)
    part_mix = lax.dynamic_slice_in_dim(merged[2], group_start, group_rows, 0)
    own_normed = lax.dynamic_slice_in_dim(normed, group_start, group_rows, 0)
    own_position = lax.dynamic_slice_in_dim(position, group_start, group_rows, 0)
    fresh_latent = jnp.dot(own_normed, latent_down, preferred_element_type=jnp.float32)
    new_latent = rms_plain(fresh_latent[:, :LATENT]).astype(jnp.bfloat16)
    new_rope = rotary(fresh_latent[:, LATENT:], own_position).astype(jnp.bfloat16)
    own_query = lax.dynamic_slice_in_dim(query_latent, group_start, group_rows, 0)
    own_rope_query = lax.dynamic_slice_in_dim(query_rope, group_start, group_rows, 0)
    own_score = jnp.einsum("thl,tl->th", own_query, new_latent, preferred_element_type=jnp.float32)
    own_score = (
        own_score
        + jnp.einsum("thr,tr->th", own_rope_query, new_rope, preferred_element_type=jnp.float32)
    ) * score_scale
    highest = jnp.maximum(part_max, own_score)
    kept_part = jnp.exp(part_max - highest)
    own_weight = jnp.exp(own_score - highest)
    denominator = part_total * kept_part + own_weight
    numerator = (
        part_mix * kept_part[..., None]
        + own_weight[..., None] * new_latent.astype(jnp.float32)[:, None, :]
    )
    attended = (numerator / denominator[..., None]).astype(jnp.bfloat16)
    heads_out = jnp.einsum(
        "thl,lhv->thv", attended, up_table[..., NOPE:], preferred_element_type=jnp.float32
    )
    heads_out = heads_out.astype(jnp.bfloat16).reshape(group_rows, head_local * VHEAD)
    partial_value = jnp.dot(heads_out, out_weight, preferred_element_type=jnp.float32)
    attn_out = lax.psum_scatter(partial_value, "expert", scatter_dimension=0, tiled=True)
    residual = hidden.astype(jnp.float32) + attn_out
    normed_ffn = rms_norm(residual, ffn_gain).astype(jnp.bfloat16)
    slots_local = expert_gate_up.shape[0]
    ff_width = expert_gate_up.shape[2]
    col_width = expert_gate_up.shape[3]
    every_row = lax.all_gather(normed_ffn, ("dp", "expert"), axis=0, tiled=True)
    my_columns = lax.dynamic_slice_in_dim(every_row, dp_index * col_width, col_width, 1)
    by_group = my_columns.reshape(dp_count, ex_count, req_local, col_width).transpose(1, 0, 2, 3)
    ffn_rows = by_group.reshape(requests, col_width)
    column_rows = lax.dynamic_index_in_dim(by_group, ex_index, 0, keepdims=False).reshape(
        dp_count * req_local, col_width
    )
    top_count = expert_ids.shape[1]
    experts_count = EXP_DEV * ex_count
    ids_order = (
        expert_ids.reshape(dp_count, ex_count, req_local, top_count)
        .transpose(1, 0, 2, 3)
        .reshape(requests, top_count)
    )
    gates_order = (
        expert_gates.reshape(dp_count, ex_count, req_local, top_count)
        .transpose(1, 0, 2, 3)
        .reshape(requests, top_count)
    )
    old_flat = old_place.reshape(-1)
    holds_map = old_flat[None, :] == jnp.arange(experts_count, dtype=jnp.int32)[:, None]
    holder = jnp.argmax(holds_map, axis=1)
    slot_of = holder[ids_order.reshape(-1)]
    capacity = 2 * requests * top_count // experts_count
    local_slot = slot_of - ex_index * slots_local
    slot_hot = local_slot[:, None] == jnp.arange(slots_local, dtype=jnp.int32)[None, :]
    slot_rank = jnp.cumsum(slot_hot.astype(jnp.int32), axis=0) - 1
    position_in = jnp.where(slot_hot, slot_rank, capacity)
    route_hot = (
        position_in[:, :, None] == jnp.arange(capacity, dtype=jnp.int32)[None, None, :]
    ).astype(jnp.float32)
    route_hot = route_hot.reshape(requests, top_count, slots_local, capacity)
    dispatch = jnp.sum(route_hot, axis=1).astype(jnp.bfloat16)
    combine = jnp.sum(route_hot * gates_order[:, :, None, None], axis=1)
    slot_inputs = jnp.einsum(
        "tsc,td->scd", dispatch, ffn_rows, preferred_element_type=jnp.float32
    ).astype(jnp.bfloat16)
    routed_part = jnp.einsum(
        "scd,sgfd->sgcf", slot_inputs, expert_gate_up, preferred_element_type=jnp.float32
    )
    shared_part = jnp.einsum(
        "td,gfd->gtf", column_rows, shared_gate_up, preferred_element_type=jnp.float32
    )
    routed_sum, shared_sum = lax.psum((routed_part, shared_part), "dp")
    activated = (jax.nn.silu(routed_sum[:, 0]) * routed_sum[:, 1]).astype(jnp.bfloat16)
    slot_out = jnp.einsum(
        "scf,sfd->scd", activated, expert_down, preferred_element_type=jnp.float32
    )
    routed = jnp.einsum("tsc,scd->td", combine, slot_out, precision=HIGHEST)
    shared_act = (jax.nn.silu(shared_sum[0]) * shared_sum[1]).astype(jnp.bfloat16)
    shared_term = jnp.dot(shared_act, shared_down, preferred_element_type=jnp.float32)
    moe_rows = lax.psum_scatter(routed, "expert", scatter_dimension=0, tiled=True)
    moe_part = lax.all_to_all(moe_rows + shared_term, "dp", split_axis=0, concat_axis=1, tiled=True)
    layer_out = (residual + moe_part).astype(jnp.bfloat16)
    changed = old_place != new_place
    moved_slot = jnp.argmax(changed, axis=1)
    wanted_expert = jnp.take_along_axis(new_place, moved_slot[:, None], axis=1)[:, 0]
    source = holder[wanted_expert]
    stacked_gate_up = expert_gate_up.reshape(slots_local, 2 * ff_width, col_width)
    spread = (
        lax.all_to_all(stacked_gate_up, "expert", split_axis=1, concat_axis=0, tiled=True),
        lax.all_to_all(expert_down, "expert", split_axis=1, concat_axis=0, tiled=True),
    )
    outgoing = (spread[0][source], spread[1][source])
    arrived = (
        lax.all_to_all(outgoing[0], "expert", split_axis=0, concat_axis=1, tiled=True),
        lax.all_to_all(outgoing[1], "expert", split_axis=0, concat_axis=1, tiled=True),
    )
    arrived_gate_up = arrived[0].reshape(1, 2, ff_width, col_width)
    my_slot = moved_slot[ex_index]
    is_moved = jnp.arange(slots_local, dtype=jnp.int32) == my_slot
    moved_gate_up = jnp.where(is_moved[:, None, None, None], arrived_gate_up, expert_gate_up)
    moved_down = jnp.where(is_moved[:, None, None], arrived[1], expert_down)
    return (layer_out, moved_gate_up, moved_down)


def solution(mesh):
    in_specs = (
        P(("dp", "expert"), None),
        P(),
        P("expert", None),
        P(),
        P(None, "expert"),
        P("expert", None),
        P("dp", None, None),
        P(),
        P(),
        P(),
        P(),
        P(),
        P(),
        P(),
        P("expert", None, None, "dp"),
        P("expert", None, "dp"),
        P(None, None, "dp"),
        P(None, "dp"),
    )
    out_specs = (P(("dp", "expert"), None), P("expert", None, None, "dp"), P("expert", None, "dp"))
    return jax.shard_map(local, mesh=mesh, in_specs=in_specs, out_specs=out_specs, check_vma=False)
```

profile of v0, /device:TPU:0, one launch (start us, length us, event | category | flops | bytes accessed | tf_op | source)
XLA Modules:
  0.0 888.6 jit_solution(454954826351109402)
XLA Ops:
  8.4 2.4 scatter_custom_fusion
  12.6 44.5 %all-gather.3 = bf16[32,1,2048]{2,1,0:T(2,128)(2,1)S(1)} all-gather(bf16[1,1,2048]{2,1,0:T(2,128)(2,1)} %bitcast.231), channel_id=1, replica_groups=mesh['dp'=4,'expert'=8] {'dp','expert'}, dimensions={0}, use_global_device_ids=true | all-gather | bytes 135168 | tf_op jit(solution)/shard_map/all_gather | solution.py:95
  59.0 2.0 fusion.86
  68.4 1.6 fusion.9
  74.7 1.5 convolution_multiply_fusion
  76.5 9.4 %all-gather.2 = f32[128,2,512]{2,0,1:T(8,128)S(1)} all-gather(f32[32,2,512]{2,0,1:T(8,128)S(1)} %fusion.24), channel_id=4, replica_groups=mesh['dp'=4,'expert'=8] {'dp'}, dimensions={0}, use_global_device_ids=true | all-gather | bytes 655360 | tf_op jit(solution)/shard_map/all_gather | solution.py:20
  86.2 8.6 all-gather.5
  96.0 7.6 all-gather.4
  104.8 13.2 %while.19 = (s32[]{:T(128)}, f32[32,2]{0,1:T(2,128)}, f32[32,2]{0,1:T(2,128)}, f32[32,2,512]{2,1,0:T(2,128)S(1)}, f32[4,32,2]{1,2,0:T(2,128)}, /*index=5*/f32[4,...) while((s32[]{:T(128)}, f32[32,2]{0,1:T(2,128)}, f32[32,2]{0,1:T(2,128)}, ...), condition=%wide.region_6.7_spmd, body=%wide.region_5.6_spmd.sunk | while | flops 98693 | bytes 659095 | solution.py:25
  106.9 1.3 copy.204
  109.2 1.3 fusion.103
  111.3 1.3 copy.204
  113.7 1.3 fusion.103
  115.7 1.3 copy.204
  118.1 2.5 fusion.29
  123.0 1.4 fusion.78
  125.3 1.3 fusion.69
  126.7 1.3 copy.134
  130.2 2.3 fusion.11
  136.4 4.4 compare_select_fusion.3
  140.9 10.5 %select_subtract_fusion = s32[192]{0:T(256)S(1)} fusion(pred[192]{0:T(512)(128)(4,1)S(1)} %get-tuple-element.241, pred[192]{0:T(512)(128)(4,1)S(1)} %get-tuple-element.240, pred[192]{0:T(512)(128)(4,1)S(1)} %get-tuple-element.239, pred[192]{0:T(512)(128)(4,1)S(1)} %get-tuple-element.238, pred[192]{0:T(512)(128)(4,1)S(1)} %get-tuple-element.237, ...), kind=kLoop, calls=%fused_computation.178 | loop fusion | flops 3456 | bytes 4872 | tf_op jit(solution)/shard_map/sub | solution.py:207
  155.6 28.0 %all-reduce.8.cloned.1.call-done = f32[8,2048]{1,0:T(8,128)} async-done(((f32[8,2048]{1,0:T(8,128)}), f32[8,2048]{1,0:T(8,128)}) %all-reduce.8.cloned.1.call-update) | async-done | bytes 65552
  183.6 2.1 multiply_reduce_fusion.1
  187.1 40.5 %all-gather.6 = bf16[32,1,2048]{2,1,0:T(2,128)(2,1)S(1)} all-gather(bf16[1,1,2048]{2,1,0:T(2,128)(2,1)S(1)} %convert_bitcast_fusion), channel_id=1, replica_groups=mesh['dp'=4,'expert'=8] {'dp','expert'}, dimensions={0}, use_global_device_ids=true | all-gather | bytes 135168 | tf_op jit(solution)/shard_map/all_gather | solution.py:183
  227.8 4.9 convolution_bitcast_fusion
  232.7 6.9 convolution_bitcast_fusion.1
  239.6 45.8 %all-reduce.12.cloned.1.call-done = (f32[2,4,2816]{2,1,0:T(4,128)}, f32[4,2,16,1408]{3,2,1,0:T(8,128)}) async-done(((f32[2,4,2816]{2,1,0:T(4,128)}, f32[4,2,16,1408]{3,2,1,0:T(8,128)}), (f32[2,4,2816]{2,1,0:T(4,128)}, f32[4,2,16,1408]{3,2,1,0:T(8,128)})) %all-reduce.12.cloned.1.call-update) | async-done | bytes 811024 | tf_op jit(solution)/shard_map/psum | solution.py:226
  285.4 3.8 fusion.21
  290.8 53.2 %all-reduce.10.cloned.1.call-done = f32[32,512]{1,0:T(8,128)} async-done(((f32[32,512]{1,0:T(8,128)}), f32[32,512]{1,0:T(8,128)}) %all-reduce.10.cloned.1.call-update) | async-done | bytes 65552
  345.8 3.6 all-to-all-start
  349.4 23.9 %copy.152 = bf16[4,1408,512]{2,0,1:T(4,128)(2,1)} copy(bf16[4,1408,512]{2,1,0:T(8,128)(2,1)} %param.35) | data formatting | bytes 11534336 | tf_op args[15]
  373.3 4.7 all-to-all-start.3
  378.0 14.4 %copy.149 = bf16[4,2,1408,512]{3,0,2,1:T(4,128)(2,1)} copy(bf16[4,2,1408,512]{3,2,1,0:T(8,128)(2,1)} %param.34) | data formatting | bytes 23068672 | tf_op args[14]
  392.4 113.3 %all-to-all-done.3 = bf16[4,1408,512]{2,0,1:T(4,128)(2,1)} async-done(((bf16[4,1408,512]{2,0,1:T(4,128)(2,1)}), bf16[4,1408,512]{2,0,1:T(4,128)(2,1)}, u32[]{:S(2)}, u32[]{:S(2)}) %all-to-all-start.3) | async-done | bytes 5767200 | tf_op jit(solution)/shard_map/all_to_all | solution.py:244
  505.7 5.4 all-to-all-start.1
  513.0 3.8 copy.153
  516.8 2.9 copy.154
  519.7 4.4 gather_fusion.5
  524.1 238.3 %all-to-all-done.1 = bf16[4,2816,512]{2,0,1:T(4,128)(2,1)} async-done(((bf16[4,2816,512]{2,0,1:T(4,128)(2,1)}), bf16[4,2816,512]{2,0,1:T(4,128)(2,1)}, u32[]{:S(2)}, u32[]{:S(2)}) %all-to-all-start.1) | async-done | bytes 11534368 | tf_op jit(solution)/shard_map/all_to_all | solution.py:243
  762.4 3.6 all-to-all-start.4
  766.0 7.9 copy.150
  773.9 5.1 copy.151
  779.0 6.6 gather_fusion.4
  785.5 15.4 %all-to-all-done.4 = bf16[8,176,512]{2,1,0:T(8,128)(2,1)S(1)} async-done(((bf16[8,176,512]{2,1,0:T(8,128)(2,1)}), bf16[8,176,512]{2,1,0:T(8,128)(2,1)S(1)}, u32[]{:S(2)}, u32[]{:S(2)}) %all-to-all-start.4) | async-done | bytes 1441824 | tf_op jit(solution)/shard_map/all_to_all | solution.py:249
  800.9 4.4 all-to-all-start.2
  807.2 5.8 broadcast_select_fusion.1
  813.0 58.2 %all-to-all-done.2 = bf16[8,352,512]{2,1,0:T(8,128)(2,1)} async-done(((bf16[8,352,512]{2,1,0:T(8,128)(2,1)}), bf16[8,352,512]{2,1,0:T(8,128)(2,1)}, u32[]{:S(2)}, u32[]{:S(2)}) %all-to-all-start.2) | async-done | bytes 2883616 | tf_op jit(solution)/shard_map/all_to_all | solution.py:248
  871.3 10.8 %broadcast_select_fusion = bf16[4,2,1408,512]{3,2,1,0:T(8,128)(2,1)} fusion(bf16[4,2,1408,512]{3,2,1,0:T(8,128)(2,1)} %param.34, pred[4]{0:T(512)(128)(4,1)S(1)} %iota_compare_fusion.7, bf16[2,1408,512]{2,1,0:T(8,128)(2,1)} %bitcast.74), kind=kLoop, calls=%fused_computation.19 | loop fusion | flops 5767168 | bytes 25952260 | tf_op jit(solution)/shard_map/jit(_where)/select_n | solution.py:254
  (152 shorter events, 47.4 us)
Async XLA Ops:
  7.2 336.8 %copy-start = (bf16[2816,512]{1,0:T(8,128)(2,1)S(1)}, bf16[2816,512]{1,0:T(8,128)(2,1)}, u32[]{:S(2)}) copy-start(bf16[2816,512]{1,0:T(8,128)(2,1)} %param.37) | copy-start | bytes 8650756
  7.2 53.9 %copy-start.15 = (s32[32]{0:T(128)S(1)}, s32[32]{0:T(128)}, u32[]{:S(2)}) copy-start(s32[32]{0:T(128)} %param.28) | copy-start | bytes 388
  7.2 176.4 %all-reduce.8.cloned.1.call-start = ((), (), s32[]{:S(2)}) async-start(), calls=%async_computation.5 | async-start | bytes 131072
  7.3 58.0 %copy-start.14 = (f32[32]{0:T(128)}, f32[32]{0:T(128)S(1)}, u32[]{:S(2)}) copy-start(f32[32]{0:T(128)S(1)} %multiply_exponential_fusion) | copy-start | bytes 388
  11.5 0.5 copy-start.10
  58.4 0.7 copy-start.5
  63.0 13.2 %copy-start.3 = (bf16[512,512]{0,1:T(8,128)(2,1)}, bf16[512,512]{0,1:T(8,128)(2,1)S(1)}, u32[]{:S(2)}) copy-start(bf16[512,512]{0,1:T(8,128)(2,1)S(1)} %copy.126) | copy-start | bytes 1572868
  66.2 0.6 copy-start.7
  66.2 0.6 copy-start.8
  68.4 7.8 copy-start.11
  71.3 14.6 %copy-start.12 = (s32[32]{0:T(128)S(1)}, s32[32]{0:T(128)}, u32[]{:S(2)}) copy-start(s32[32]{0:T(128)} %copy-done.10) | copy-start | bytes 388
  118.1 12.1 %copy-start.4 = (bf16[512,512]{0,1:T(8,128)(2,1)S(1)}, bf16[512,512]{0,1:T(8,128)(2,1)}, u32[]{:S(2)}) copy-start(bf16[512,512]{0,1:T(8,128)(2,1)} %copy-done.3) | copy-start | bytes 1572868
  120.5 0.6 copy-start.6
  132.5 153.0 %all-reduce.12.cloned.1.call-start = ((), (), s32[]{:S(2)}) async-start(), calls=%async_computation.7 | async-start | bytes 1622016 | tf_op jit(solution)/shard_map/psum | solution.py:226
  239.6 104.4 %all-reduce.10.cloned.1.call-start = ((), (), s32[]{:S(2)}) async-start(), calls=%async_computation.6 | async-start | bytes 131072
  285.4 58.5 %copy-start.9 = (f32[2,4,2816]{2,1,0:T(4,128)S(1)}, f32[2,4,2816]{2,1,0:T(4,128)}, u32[]{:S(2)}) copy-start(f32[2,4,2816]{2,1,0:T(4,128)} %get-tuple-element.256) | copy-start | bytes 270340
  345.8 27.5 %all-to-all-start = ((f32[4,1,512]{2,1,0:T(1,128)}), f32[4,1,512]{2,1,0:T(1,128)S(1)}, u32[]{:S(2)}, u32[]{:S(2)}) async-start(f32[4,1,512]{2,1,0:T(1,128)} %copy.148), calls=%async_computation | async-start | bytes 16384 | tf_op jit(solution)/shard_map/all_to_all | solution.py:235
  373.3 132.4 %all-to-all-start.3 = ((bf16[4,1408,512]{2,0,1:T(4,128)(2,1)}), bf16[4,1408,512]{2,0,1:T(4,128)(2,1)}, u32[]{:S(2)}, u32[]{:S(2)}) async-start(bf16[4,1408,512]{2,0,1:T(4,128)(2,1)} %copy.152), calls=%async_computation.3 | async-start | bytes 11534336 | tf_op jit(solution)/shard_map/all_to_all | solution.py:244
  505.7 5.4 copy-start.2
  505.7 5.4 copy-start.13
  505.7 256.7 %all-to-all-start.1 = ((bf16[4,2816,512]{2,0,1:T(4,128)(2,1)}), bf16[4,2816,512]{2,0,1:T(4,128)(2,1)}, u32[]{:S(2)}, u32[]{:S(2)}) async-start(bf16[4,2816,512]{2,0,1:T(4,128)(2,1)} %bitcast.217), calls=%async_computation.1 | async-start | bytes 23068672 | tf_op jit(solution)/shard_map/all_to_all | solution.py:243
  762.4 38.5 %all-to-all-start.4 = ((bf16[8,176,512]{2,1,0:T(8,128)(2,1)}), bf16[8,176,512]{2,1,0:T(8,128)(2,1)S(1)}, u32[]{:S(2)}, u32[]{:S(2)}) async-start(bf16[8,176,512]{2,1,0:T(8,128)(2,1)} %gather_fusion.5), calls=%async_computation.4 | async-start | bytes 2883584 | tf_op jit(solution)/shard_map/all_to_all | solution.py:249
  800.9 70.4 %all-to-all-start.2 = ((bf16[8,352,512]{2,1,0:T(8,128)(2,1)}), bf16[8,352,512]{2,1,0:T(8,128)(2,1)}, u32[]{:S(2)}, u32[]{:S(2)}) async-start(bf16[8,352,512]{2,1,0:T(8,128)(2,1)} %gather_fusion.4), calls=%async_computation.2 | async-start | bytes 5767168 | tf_op jit(solution)/shard_map/all_to_all | solution.py:248
  871.3 10.8 %copy-start.1 = (bf16[2816,512]{1,0:T(8,128)(2,1)S(1)}, bf16[2816,512]{1,0:T(8,128)(2,1)}, u32[]{:S(2)}) copy-start(bf16[2816,512]{1,0:T(8,128)(2,1)} %param.37) | copy-start | bytes 8650756
Sparse Core Ops, SparseCore 0:
  132.6 50.9 all-reduce.7
  239.7 45.6 all-reduce.11
  290.2 53.6 all-reduce.9
where the time goes:
time: 891 us; the launch traced here: 889 us
  waiting for transfers between devices  552 us (62%)
  blocking collectives  111 us (12%)
  local copies, waits for them, and re-layouts  100 us (11%)
  other arithmetic  57 us (6%)
  matrix products  31 us (3%)
  starting transfers between devices  21.9 us (2%)
  between operations  15.5 us (2%)
    all_to_all x1, waiting for transfers between devices, local(): lax.all_to_all(stacked_gate_up, 'expert', split_axis=1, concat_axis=0, ti...  238 us
    all_to_all x1, waiting for transfers between devices, local(): lax.all_to_all(expert_down, 'expert', split_axis=1, concat_axis=0, tiled=...  113 us
    unnamed x5, waiting for transfers between devices  81.2 us
    all_to_all x1, waiting for transfers between devices, local(): lax.all_to_all(outgoing[0], 'expert', split_axis=0, concat_axis=1, tiled=...  58.2 us
    psum x1, waiting for transfers between devices, local(): routed_sum, shared_sum = lax.psum((routed_part, shared_part), 'dp')  45.8 us
    unnamed x41, local copies, waits for them, and re-layouts  44.8 us
    all_gather x1, blocking collectives, local(): everyone = lax.all_gather(hidden, ('dp', 'expert'), axis=0, tiled=True)  44.5 us
    all_gather x1, blocking collectives, local(): every_row = lax.all_gather(normed_ffn, ('dp', 'expert'), axis=0, tiled=True)  40.5 us
  transfers between devices with their start and end apart: 8, of which 7 were waited for; matrix products, arithmetic and copies ran while one was open for 11% of the time, Pallas kernels for 0%

commit v1 on v0

--- a/solution.py
+++ b/solution.py
@@ -14,6 +14,22 @@
 ROPE_BASE = 50000.0
 MASKED_SCORE = -1e30
 HIGHEST = lax.Precision.HIGHEST
+
+
+def swapped_with_each(array, axis, split, join):
+    ways, here = (lax.axis_size(axis), lax.axis_index(axis))
+    width = array.shape[split] // ways
+    shape = list(array.shape)
+    shape[split] = width
+    height = shape[join]
+    shape[join] = height * ways
+    full = jnp.zeros(shape, array.dtype)
+    for mask in range(ways):
+        part = lax.dynamic_slice_in_dim(array, (here ^ mask) * width, width, axis=split)
+        if mask:
+            part = lax.ppermute(part, axis, [(d, d ^ mask) for d in range(ways)])
+        full = lax.dynamic_update_slice_in_dim(full, part, (here ^ mask) * height, axis=join)
+    return full
 
 
 def combined_all(part, axis, combine):
@@ -241,7 +257,7 @@
     stacked_gate_up = expert_gate_up.reshape(slots_local, 2 * ff_width, col_width)
     spread = (
         lax.all_to_all(stacked_gate_up, "expert", split_axis=1, concat_axis=0, tiled=True),
-        lax.all_to_all(expert_down, "expert", split_axis=1, concat_axis=0, tiled=True),
+        swapped_with_each(expert_down, "expert", 1, 0),
     )
     outgoing = (spread[0][source], spread[1][source])
     arrived = (

time: 891 us -> 857 us (0.962)
  starting transfers between devices: 21.9 us -> 55.6 us
  waiting for transfers between devices: 552 us -> 519 us
  local copies, waits for them, and re-layouts: 100 us -> 78.9 us
  other arithmetic: 57 us -> 47.3 us
    ppermute x0 -> x7, waiting for transfers between devices: none -> 316 us  [swapped_with_each(): part = lax.ppermute(part, axis, [(d, d ^ mask) for d in range(ways)])]
    all_to_all x1, waiting for transfers between devices: 238 us -> 0.01 us  [local(): lax.all_to_all(stacked_gate_up, 'expert', split_axis=1, concat_axis=0, ti...]
    all_to_all x1 -> x0, waiting for transfers between devices: 113 us -> none  [local(): lax.all_to_all(expert_down, 'expert', split_axis=1, concat_axis=0, tiled=...]
    all_to_all x1, starting transfers between devices: 3.58 us -> 31.1 us  [local(): lax.all_to_all(outgoing[1], 'expert', split_axis=0, concat_axis=1, tiled=...]
    unnamed x41 -> x46, local copies, waits for them, and re-layouts: 44.8 us -> 20 us
    ppermute x0 -> x7, starting transfers between devices: none -> 10.8 us  [swapped_with_each(): part = lax.ppermute(part, axis, [(d, d ^ mask) for d in range(ways)])]
  transfers between devices with their start and end apart: 8 -> 14, of which waited for: 7 -> 9; matrix products, arithmetic and copies ran while one was open for 11% -> 10% of each run, Pallas kernels for 0% -> 0%
where the time goes in v1:
time: 857 us; the launch traced here: 855 us
  waiting for transfers between devices  519 us (61%)
  blocking collectives  109 us (13%)
  local copies, waits for them, and re-layouts  78.9 us (9%)
  starting transfers between devices  55.6 us (6%)
  other arithmetic  47.3 us (6%)
  matrix products  29.7 us (3%)
  between operations  15.6 us (2%)
    ppermute x7, waiting for transfers between devices, swapped_with_each(): part = lax.ppermute(part, axis, [(d, d ^ mask) for d in range(ways)])  316 us
    unnamed x5, waiting for transfers between devices  82.6 us
    all_to_all x1, waiting for transfers between devices, local(): lax.all_to_all(outgoing[0], 'expert', split_axis=0, concat_axis=1, tiled=...  58.3 us
    psum x1, waiting for transfers between devices, local(): routed_sum, shared_sum = lax.psum((routed_part, shared_part), 'dp')  45.8 us
    all_gather x1, blocking collectives, local(): everyone = lax.all_gather(hidden, ('dp', 'expert'), axis=0, tiled=True)  44.5 us
    all_gather x1, blocking collectives, local(): every_row = lax.all_gather(normed_ffn, ('dp', 'expert'), axis=0, tiled=True)  40.5 us
    all_to_all x1, starting transfers between devices, local(): lax.all_to_all(outgoing[1], 'expert', split_axis=0, concat_axis=1, tiled=...  31.1 us
    all_gather x3, blocking collectives, combined_all(): gathered = jax.tree.map(lambda a: lax.all_gather(a, axis), part)  24.2 us
  transfers between devices with their start and end apart: 14, of which 9 were waited for; matrix products, arithmetic and copies ran while one was open for 10% of the time, Pallas kernels for 0%

profile of v1, /device:TPU:0, one launch (start us, length us, event | category | flops | bytes accessed | tf_op | source)
XLA Modules:
  0.0 855.0 jit_solution(16270287530988068560)
XLA Ops:
  9.0 2.4 scatter_custom_fusion
  13.3 44.5 %all-gather.3 = bf16[32,1,2048]{2,1,0:T(2,128)(2,1)S(1)} all-gather(bf16[1,1,2048]{2,1,0:T(2,128)(2,1)} %bitcast.225), channel_id=1, replica_groups=mesh['dp'=4,'expert'=8] {'dp','expert'}, dimensions={0}, use_global_device_ids=true | all-gather | bytes 135168 | tf_op jit(solution)/shard_map/all_gather | solution.py:111
  59.7 2.0 fusion.85
  66.5 1.4 multiply_cosine_fusion
  67.9 1.5 gather_fusion
  71.6 1.6 fusion.9
  74.9 7.1 all-gather.4
  83.5 1.6 convolution_multiply_fusion
  85.3 8.1 all-gather.5
  93.6 9.0 %all-gather.2 = f32[128,2,512]{2,0,1:T(8,128)S(1)} all-gather(f32[32,2,512]{2,0,1:T(8,128)S(1)} %fusion.24), channel_id=4, replica_groups=mesh['dp'=4,'expert'=8] {'dp'}, dimensions={0}, use_global_device_ids=true | all-gather | bytes 655360 | tf_op jit(solution)/shard_map/all_gather | solution.py:36
  103.4 4.2 while.19
  107.6 2.4 fusion.29
  112.1 2.3 fusion.11
  118.3 4.4 compare_select_fusion.3
  122.9 10.5 %select_subtract_fusion = s32[192]{0:T(256)S(1)} fusion(pred[192]{0:T(512)(128)(4,1)S(1)} %get-tuple-element.241, pred[192]{0:T(512)(128)(4,1)S(1)} %get-tuple-element.240, pred[192]{0:T(512)(128)(4,1)S(1)} %get-tuple-element.239, pred[192]{0:T(512)(128)(4,1)S(1)} %get-tuple-element.238, pred[192]{0:T(512)(128)(4,1)S(1)} %get-tuple-element.237, ...), kind=kLoop, calls=%fused_computation.192 | loop fusion | flops 3456 | bytes 4872 | tf_op jit(solution)/shard_map/sub | solution.py:223
  136.2 29.4 %all-reduce.8.cloned.1.call-done = f32[8,2048]{1,0:T(8,128)} async-done(((f32[8,2048]{1,0:T(8,128)}), f32[8,2048]{1,0:T(8,128)}) %all-reduce.8.cloned.1.call-update) | async-done | bytes 65552
  165.6 2.1 multiply_reduce_fusion.1
  168.4 40.5 %all-gather.6 = bf16[32,1,2048]{2,1,0:T(2,128)(2,1)S(1)} all-gather(bf16[1,1,2048]{2,1,0:T(2,128)(2,1)S(1)} %convert_bitcast_fusion), channel_id=1, replica_groups=mesh['dp'=4,'expert'=8] {'dp','expert'}, dimensions={0}, use_global_device_ids=true | all-gather | bytes 135168 | tf_op jit(solution)/shard_map/all_gather | solution.py:199
  209.2 4.9 convolution_bitcast_fusion
  214.0 6.9 convolution_bitcast_fusion.1
  221.0 45.8 %all-reduce.12.cloned.1.call-done = (f32[2,4,2816]{2,1,0:T(4,128)}, f32[4,2,16,1408]{3,2,1,0:T(8,128)}) async-done(((f32[2,4,2816]{2,1,0:T(4,128)}, f32[4,2,16,1408]{3,2,1,0:T(8,128)}), (f32[2,4,2816]{2,1,0:T(4,128)}, f32[4,2,16,1408]{3,2,1,0:T(8,128)})) %all-reduce.12.cloned.1.call-update) | async-done | bytes 811024 | tf_op jit(solution)/shard_map/psum | solution.py:242
  266.8 3.8 fusion.21
  272.1 53.2 %all-reduce.10.cloned.1.call-done = f32[32,512]{1,0:T(8,128)} async-done(((f32[32,512]{1,0:T(8,128)}), f32[32,512]{1,0:T(8,128)}) %all-reduce.10.cloned.1.call-update) | async-done | bytes 65552
  327.1 3.6 all-to-all-start
  330.7 14.4 %copy.145 = bf16[4,2,1408,512]{3,0,2,1:T(4,128)(2,1)} copy(bf16[4,2,1408,512]{3,2,1,0:T(8,128)(2,1)} %param.34) | data formatting | bytes 23068672 | tf_op args[14]
  345.2 5.4 all-to-all-start.1
  350.7 3.2 broadcast_in_dim.156
  353.8 5.2 constant_dynamic-slice_fusion.2
  359.4 1.7 collective-permute-start.1
  361.1 2.6 collective-permute-start.3
  365.7 3.6 collective-permute-start.5
  369.3 183.5 %collective-permute-done.1 = bf16[4,176,512]{2,1,0:T(8,128)(2,1)} collective-permute-done((bf16[4,176,512]{2,1,0:T(8,128)(2,1)}, bf16[4,176,512]{2,1,0:T(8,128)(2,1)}, u32[]{:S(2)}, u32[]{:S(2)}) %collective-permute-start.1) | collective-permute-done | bytes 720928 | tf_op jit(solution)/shard_map/ppermute | solution.py:30
  552.9 2.5 collective-permute-start.6
  555.3 2.0 constant_dynamic-update-slice_fusion.6
  557.4 2.0 constant_dynamic-update-slice_fusion.5
  559.4 8.9 %collective-permute-done.2 = bf16[4,176,512]{2,1,0:T(8,128)(2,1)S(1)} collective-permute-done((bf16[4,176,512]{2,1,0:T(8,128)(2,1)}, bf16[4,176,512]{2,1,0:T(8,128)(2,1)S(1)}, u32[]{:S(2)}, u32[]{:S(2)}) %collective-permute-start.2) | collective-permute-done | bytes 720928 | tf_op jit(solution)/shard_map/ppermute | solution.py:30
  569.2 110.3 %collective-permute-done.3 = bf16[4,176,512]{2,1,0:T(8,128)(2,1)S(1)} collective-permute-done((bf16[4,176,512]{2,1,0:T(8,128)(2,1)}, bf16[4,176,512]{2,1,0:T(8,128)(2,1)S(1)}, u32[]{:S(2)}, u32[]{:S(2)}) %collective-permute-start.3) | collective-permute-done | bytes 720928 | tf_op jit(solution)/shard_map/ppermute | solution.py:30
  680.4 13.6 %collective-permute-done.4 = bf16[4,176,512]{2,1,0:T(8,128)(2,1)S(1)} collective-permute-done((bf16[4,176,512]{2,1,0:T(8,128)(2,1)}, bf16[4,176,512]{2,1,0:T(8,128)(2,1)S(1)}, u32[]{:S(2)}, u32[]{:S(2)}) %collective-permute-start.4) | collective-permute-done | bytes 720928 | tf_op jit(solution)/shard_map/ppermute | solution.py:30
  696.7 4.4 gather_fusion.5
  701.1 31.1 %all-to-all-start.3 = ((bf16[8,176,512]{2,1,0:T(8,128)(2,1)}), bf16[8,176,512]{2,1,0:T(8,128)(2,1)S(1)}, u32[]{:S(2)}, u32[]{:S(2)}) async-start(bf16[8,176,512]{2,1,0:T(8,128)(2,1)} %gather_fusion.5), calls=%async_computation.3 | async-start | bytes 2883584 | tf_op jit(solution)/shard_map/all_to_all | solution.py:265
  732.3 7.9 copy.146
  740.2 5.1 copy.147
  745.3 6.6 gather_fusion.4
  751.9 15.4 %all-to-all-done.3 = bf16[8,176,512]{2,1,0:T(8,128)(2,1)S(1)} async-done(((bf16[8,176,512]{2,1,0:T(8,128)(2,1)}), bf16[8,176,512]{2,1,0:T(8,128)(2,1)S(1)}, u32[]{:S(2)}, u32[]{:S(2)}) %all-to-all-start.3) | async-done | bytes 1441824 | tf_op jit(solution)/shard_map/all_to_all | solution.py:265
  767.3 4.4 all-to-all-start.2
  773.6 5.8 broadcast_select_fusion.1
  779.4 58.3 %all-to-all-done.2 = bf16[8,352,512]{2,1,0:T(8,128)(2,1)} async-done(((bf16[8,352,512]{2,1,0:T(8,128)(2,1)}), bf16[8,352,512]{2,1,0:T(8,128)(2,1)}, u32[]{:S(2)}, u32[]{:S(2)}) %all-to-all-start.2) | async-done | bytes 2883616 | tf_op jit(solution)/shard_map/all_to_all | solution.py:264
  837.7 10.8 %broadcast_select_fusion = bf16[4,2,1408,512]{3,2,1,0:T(8,128)(2,1)} fusion(bf16[4,2,1408,512]{3,2,1,0:T(8,128)(2,1)} %param.34, pred[4]{0:T(512)(128)(4,1)S(1)} %iota_compare_fusion.7, bf16[2,1408,512]{2,1,0:T(8,128)(2,1)} %bitcast.74), kind=kLoop, calls=%fused_computation.19 | loop fusion | flops 5767168 | bytes 25952260 | tf_op jit(solution)/shard_map/jit(_where)/select_n | solution.py:270
  (176 shorter events, 41.4 us)
Async XLA Ops:
  7.2 318.1 %copy-start = (bf16[2816,512]{1,0:T(8,128)(2,1)S(1)}, bf16[2816,512]{1,0:T(8,128)(2,1)}, u32[]{:S(2)}) copy-start(bf16[2816,512]{1,0:T(8,128)(2,1)} %param.37) | copy-start | bytes 8650756
  7.2 158.4 %all-reduce.8.cloned.1.call-start = ((), (), s32[]{:S(2)}) async-start(), calls=%async_computation.4 | async-start | bytes 131072
  11.5 63.3 %copy-start.16 = (pred[32]{0:T(512)(128)(4,1)}, pred[32]{0:T(512)(128)(4,1)S(1)}, u32[]{:S(2)}) copy-start(pred[32]{0:T(512)(128)(4,1)S(1)} %get-tuple-element.269) | copy-start | bytes 100
  13.3 89.3 %copy-start.4 = (bf16[512,512]{0,1:T(8,128)(2,1)}, bf16[512,512]{0,1:T(8,128)(2,1)S(1)}, u32[]{:S(2)}) copy-start(bf16[512,512]{0,1:T(8,128)(2,1)S(1)} %copy.122) | copy-start | bytes 1572868
  59.1 0.6 copy-start.5
  63.4 8.2 copy-start.15
  70.3 0.6 copy-start.6
  70.3 0.6 copy-start.8
  73.2 37.8 %copy-start.7 = (bf16[32,2,32]{2,1,0:T(2,128)(2,1)S(1)}, bf16[32,2,32]{2,1,0:T(2,128)(2,1)}, u32[]{:S(2)}) copy-start(bf16[32,2,32]{2,1,0:T(2,128)(2,1)} %copy-done.6) | copy-start | bytes 12292
  73.2 37.8 %copy-start.9 = (bf16[32,2,32]{2,1,0:T(2,128)(2,1)S(1)}, bf16[32,2,32]{2,1,0:T(2,128)(2,1)}, u32[]{:S(2)}) copy-start(bf16[32,2,32]{2,1,0:T(2,128)(2,1)} %copy-done.8) | copy-start | bytes 12292
  83.5 82.1 %copy-start.10 = (bf16[1,2048]{1,0:T(2,128)(2,1)S(1)}, bf16[1,2048]{1,0:T(2,128)(2,1)}, u32[]{:S(2)}) copy-start(bf16[1,2048]{1,0:T(2,128)(2,1)} %param.20) | copy-start | bytes 12292
  85.1 26.3 %copy-start.12 = (bf16[8,2,512]{2,0,1:T(8,128)(2,1)S(1)}, bf16[8,2,512]{2,0,1:T(8,128)(2,1)}, u32[]{:S(2)}) copy-start(bf16[8,2,512]{2,0,1:T(8,128)(2,1)} %dynamic-slice_bitcast_fusion) | copy-start | bytes 49156
  85.1 50.2 %copy-start.17 = (f32[32,6]{0,1:T(8,128)S(1)}, f32[32,6]{0,1:T(8,128)}, u32[]{:S(2)}) copy-start(f32[32,6]{0,1:T(8,128)} %param.31) | copy-start | bytes 2308
  85.1 50.5 %copy-start.18 = (u32[32]{0:T(128)S(1)}, u32[32]{0:T(128)}, u32[]{:S(2)}) copy-start(u32[32]{0:T(128)} %constant.215) | copy-start | bytes 388
  85.1 83.3 %copy-start.13 = (f32[2048]{0:T(1024)S(1)}, f32[2048]{0:T(1024)}, u32[]{:S(2)}) copy-start(f32[2048]{0:T(1024)} %param.29) | copy-start | bytes 24580
  102.6 0.8 copy-start.3
  114.4 152.3 %all-reduce.12.cloned.1.call-start = ((), (), s32[]{:S(2)}) async-start(), calls=%async_computation.6 | async-start | bytes 1622016 | tf_op jit(solution)/shard_map/psum | solution.py:242
  220.9 104.4 %all-reduce.10.cloned.1.call-start = ((), (), s32[]{:S(2)}) async-start(), calls=%async_computation.5 | async-start | bytes 131072
  266.8 58.5 %copy-start.11 = (f32[2,4,2816]{2,1,0:T(4,128)S(1)}, f32[2,4,2816]{2,1,0:T(4,128)}, u32[]{:S(2)}) copy-start(f32[2,4,2816]{2,1,0:T(4,128)} %get-tuple-element.256) | copy-start | bytes 270340
  327.1 18.1 %all-to-all-start = ((f32[4,1,512]{2,1,0:T(1,128)}), f32[4,1,512]{2,1,0:T(1,128)S(1)}, u32[]{:S(2)}, u32[]{:S(2)}) async-start(f32[4,1,512]{2,1,0:T(1,128)} %copy.144), calls=%async_computation | async-start | bytes 16384 | tf_op jit(solution)/shard_map/all_to_all | solution.py:251
  345.2 356.0 %all-to-all-start.1 = ((bf16[4,2816,512]{2,0,1:T(4,128)(2,1)}), bf16[4,2816,512]{2,0,1:T(4,128)(2,1)}, u32[]{:S(2)}, u32[]{:S(2)}) async-start(bf16[4,2816,512]{2,0,1:T(4,128)(2,1)} %bitcast.213), calls=%async_computation.1 | async-start | bytes 23068672 | tf_op jit(solution)/shard_map/all_to_all | solution.py:259
  353.8 9.9 %copy-start.2 = (s32[8,4]{0,1:T(4,128)S(1)}, s32[8,4]{0,1:T(4,128)}, u32[]{:S(2)}) copy-start(s32[8,4]{0,1:T(4,128)} %param.33) | copy-start | bytes 388
  353.8 9.9 %copy-start.14 = (s32[8,4]{0,1:T(4,128)S(1)}, s32[8,4]{0,1:T(4,128)}, u32[]{:S(2)}) copy-start(s32[8,4]{0,1:T(4,128)} %param.32) | copy-start | bytes 388
  359.0 6.7 collective-permute-start
  359.4 193.5 %collective-permute-start.1 = (bf16[4,176,512]{2,1,0:T(8,128)(2,1)}, bf16[4,176,512]{2,1,0:T(8,128)(2,1)}, u32[]{:S(2)}, u32[]{:S(2)}) collective-permute-start(bf16[4,176,512]{2,1,0:T(8,128)(2,1)} %get-tuple-element.276), channel_id=1, source_target_pairs={{0,2},{1,3},{2,0},{3,1},{4,6},{5,7},{6,4},{7,5},{8,10},{9,11},{10,... | collective-permute-start | bytes 2162696 | tf_op jit(solution)/shard_map/ppermute | solution.py:30
  361.1 207.2 %collective-permute-start.2 = (bf16[4,176,512]{2,1,0:T(8,128)(2,1)}, bf16[4,176,512]{2,1,0:T(8,128)(2,1)S(1)}, u32[]{:S(2)}, u32[]{:S(2)}) collective-permute-start(bf16[4,176,512]{2,1,0:T(8,128)(2,1)} %get-tuple-element.275), channel_id=1, source_target_pairs={{0,3},{1,2},{2,1},{3,0},{4,7},{5,6},{6,5},{7,4},{8,11},{9,10},{10,... | collective-permute-start | bytes 2162696 | tf_op jit(solution)/shard_map/ppermute | solution.py:30
  361.1 318.4 %collective-permute-start.3 = (bf16[4,176,512]{2,1,0:T(8,128)(2,1)}, bf16[4,176,512]{2,1,0:T(8,128)(2,1)S(1)}, u32[]{:S(2)}, u32[]{:S(2)}) collective-permute-start(bf16[4,176,512]{2,1,0:T(8,128)(2,1)} %get-tuple-element.274), channel_id=1, source_target_pairs={{0,4},{1,5},{2,6},{3,7},{4,0},{5,1},{6,2},{7,3},{8,12},{9,13},{10,... | collective-permute-start | bytes 2162696 | tf_op jit(solution)/shard_map/ppermute | solution.py:30
  363.7 330.3 %collective-permute-start.4 = (bf16[4,176,512]{2,1,0:T(8,128)(2,1)}, bf16[4,176,512]{2,1,0:T(8,128)(2,1)S(1)}, u32[]{:S(2)}, u32[]{:S(2)}) collective-permute-start(bf16[4,176,512]{2,1,0:T(8,128)(2,1)} %get-tuple-element.273), channel_id=1, source_target_pairs={{0,5},{1,4},{2,7},{3,6},{4,1},{5,0},{6,3},{7,2},{8,13},{9,12},{10,... | collective-permute-start | bytes 2162696 | tf_op jit(solution)/shard_map/ppermute | solution.py:30
  365.7 329.2 %collective-permute-start.5 = (bf16[4,176,512]{2,1,0:T(8,128)(2,1)}, bf16[4,176,512]{2,1,0:T(8,128)(2,1)S(1)}, u32[]{:S(2)}, u32[]{:S(2)}) collective-permute-start(bf16[4,176,512]{2,1,0:T(8,128)(2,1)} %get-tuple-element.272), channel_id=1, source_target_pairs={{0,6},{1,7},{2,4},{3,5},{4,2},{5,3},{6,0},{7,1},{8,14},{9,15},{10,... | collective-permute-start | bytes 2162696 | tf_op jit(solution)/shard_map/ppermute | solution.py:30
  552.9 143.0 %collective-permute-start.6 = (bf16[4,176,512]{2,1,0:T(8,128)(2,1)}, bf16[4,176,512]{2,1,0:T(8,128)(2,1)S(1)}, u32[]{:S(2)}, u32[]{:S(2)}) collective-permute-start(bf16[4,176,512]{2,1,0:T(8,128)(2,1)} %get-tuple-element.271), channel_id=1, source_target_pairs={{0,7},{1,6},{2,5},{3,4},{4,3},{5,2},{6,1},{7,0},{8,15},{9,14},{10,... | collective-permute-start | bytes 2162696 | tf_op jit(solution)/shard_map/ppermute | solution.py:30
  701.1 66.1 %all-to-all-start.3 = ((bf16[8,176,512]{2,1,0:T(8,128)(2,1)}), bf16[8,176,512]{2,1,0:T(8,128)(2,1)S(1)}, u32[]{:S(2)}, u32[]{:S(2)}) async-start(bf16[8,176,512]{2,1,0:T(8,128)(2,1)} %gather_fusion.5), calls=%async_computation.3 | async-start | bytes 2883584 | tf_op jit(solution)/shard_map/all_to_all | solution.py:265
  767.3 70.4 %all-to-all-start.2 = ((bf16[8,352,512]{2,1,0:T(8,128)(2,1)}), bf16[8,352,512]{2,1,0:T(8,128)(2,1)}, u32[]{:S(2)}, u32[]{:S(2)}) async-start(bf16[8,352,512]{2,1,0:T(8,128)(2,1)} %gather_fusion.4), calls=%async_computation.2 | async-start | bytes 5767168 | tf_op jit(solution)/shard_map/all_to_all | solution.py:264
  837.7 10.8 %copy-start.1 = (bf16[2816,512]{1,0:T(8,128)(2,1)S(1)}, bf16[2816,512]{1,0:T(8,128)(2,1)}, u32[]{:S(2)}) copy-start(bf16[2816,512]{1,0:T(8,128)(2,1)} %param.37) | copy-start | bytes 8650756
Sparse Core Ops, SparseCore 0:
  114.6 51.0 all-reduce.7
  221.0 45.6 all-reduce.11
  271.6 53.6 all-reduce.9
